TPU v7x, 512 devices: a whole 4x8x8 slice. The times are simulated.
512 devices in a mesh: grp: 16 (over x_lo, z), seq: 32 (over y, x_hi, core).
Axes of the slice: x: 4 (x_hi: 2, x_lo: 2; x = x_hi * 2 + x_lo), y: 8, z: 8, core: 2. Of those that a mesh axis runs over, the one named last changes fastest.
Arguments:
- signal: bfloat16 [131072, 256], P(('grp', 'seq')), may hold values from -6 to 6
- cotangent: bfloat16 [131072, 256], P(('grp', 'seq')), may hold values from -6 to 6
- w_taps: bfloat16 [512, 1024], replicated, may hold values from -0.25 to 0.25
- gate_bias: float32 [1024], replicated, may hold values from -3 to 3
- w_out: bfloat16 [512, 256], replicated, may hold values from -0.25 to 0.25
Outputs:
- block_out: bfloat16 [131072, 256], P(('grp', 'seq'))
- grad_in: bfloat16 [131072, 256], P(('grp', 'seq'))
- grad_taps: float32 [512, 1024], P('seq')
- grad_bias: float32 [1024], P('seq')
- grad_out: float32 [512, 256], P('seq')
All inputs are finite; a program needn't handle non-finite values.
Results may differ from a plain program's by a relative error of at most 0.0045.
Values may be sent and summed in bfloat16 or wider, within the bound.
No kernel may reach another device: no remote copies, remote signals or barrier semaphores. Data moves between devices by JAX's collectives and lax.ppermute only.
A program may use at most 64 MiB of HBM per device.

v0:
```python
import jax
import jax.numpy as jnp
from jax import lax
from jax.sharding import PartitionSpec as P


def from_behind(array, axis, by):
    count = lax.axis_size(axis)
    pairs = [(i, i + by) for i in range(count) if 0 <= i + by < count]
    return lax.ppermute(array, axis, pairs)


def reduced_row_axes(left, right):
    return lax.dot_general(
        left, right, (((0,), (0,)), ((), ())), preferred_element_type=jnp.float32
    )


def contract_cols(left, right):
    return lax.dot_general(
        left, right, (((1,), (1,)), ((), ())), preferred_element_type=jnp.float32
    )


def per_device(signal, cotangent, w_taps, gate_bias, w_out):
    width = signal.shape[1]
    units = w_out.shape[0]
    lagged_input = from_behind(signal, ("grp", "seq"), 2)
    preact = jnp.dot(signal, w_taps[width:], preferred_element_type=jnp.float32)
    preact = (
        preact
        + jnp.dot(lagged_input, w_taps[:width], preferred_element_type=jnp.float32)
        + gate_bias
    )
    squashed = jnp.tanh(preact[:, :units])
    opened = jax.nn.sigmoid(preact[:, units:])
    hidden_state = (squashed * opened).astype(jnp.bfloat16)
    block_out = (
        signal.astype(jnp.float32)
        + jnp.dot(hidden_state, w_out, preferred_element_type=jnp.float32)
    ).astype(jnp.bfloat16)
    grad_hidden = contract_cols(cotangent, w_out)
    grad_pre = jnp.concatenate(
        [
            grad_hidden * opened * (1.0 - squashed * squashed),
            grad_hidden * squashed * opened * (1.0 - opened),
        ],
        axis=1,
    ).astype(jnp.bfloat16)
    part_out = reduced_row_axes(hidden_state, cotangent)
    part_taps = jnp.concatenate(
        [reduced_row_axes(lagged_input, grad_pre), reduced_row_axes(signal, grad_pre)], axis=0
    )
    part_bias = jnp.sum(grad_pre.astype(jnp.float32), axis=0)
    later_pre = from_behind(grad_pre, ("grp", "seq"), -2)
    tapped_signal = contract_cols(later_pre, w_taps[:width])
    nearby = cotangent.astype(jnp.float32) + contract_cols(grad_pre, w_taps[width:])
    grad_in = (nearby + tapped_signal).astype(jnp.bfloat16)
    groups = lax.axis_size("seq")
    lanes = 128
    rows_taps = part_taps.shape[0] // groups
    rows_out = part_out.shape[0] // groups
    share_bias = part_bias.shape[0] // groups
    taps_r = rows_taps * part_taps.shape[1] // lanes
    out_r = rows_out * part_out.shape[1] // lanes
    bias_r = 8
    bias_rows = jnp.pad(
        part_bias.reshape(groups, 1, share_bias), ((0, 0), (0, bias_r), (0, lanes - share_bias))
    )[:, :bias_r]
    packed = jnp.concatenate(
        [
            part_taps.reshape(groups, taps_r, lanes),
            part_out.reshape(groups, out_r, lanes),
            bias_rows,
        ],
        axis=1,
    ).reshape(groups * (taps_r + out_r + bias_r), lanes)
    mine = lax.psum_scatter(packed, "seq", scatter_dimension=0, tiled=True)
    mine = lax.psum(mine, "grp")
    grad_taps = mine[:taps_r].reshape(rows_taps, part_taps.shape[1])
    grad_out = mine[taps_r : taps_r + out_r].reshape(rows_out, part_out.shape[1])
    grad_bias = mine[taps_r + out_r, :share_bias]
    return (block_out, grad_in, grad_taps, grad_bias, grad_out)


def solution(mesh):
    placed = (P(("grp", "seq"), None), P(("grp", "seq"), None), P(), P(), P())
    return jax.shard_map(
        per_device,
        mesh=mesh,
        in_specs=placed,
        out_specs=(
            P(("grp", "seq"), None),
            P(("grp", "seq"), None),
            P("seq", None),
            P("seq"),
            P("seq", None),
        ),
        check_vma=False,
    )
```

profile of v0, /device:TPU:6, one launch (start us, length us, event | category | flops | bytes accessed | tf_op | source)
XLA Modules:
  0.0 307.3 jit_solution(14182650442721048356)
XLA Ops:
  7.2 0.0 copy-start
  7.2 0.0 reduce-scatter.4.cloned.1.call-start
  7.2 4.5 %collective-permute-start = (bf16[256,256]{1,0:T(8,128)(2,1)}, bf16[256,256]{1,0:T(8,128)(2,1)S(1)}, u32[]{:S(2)}, u32[]{:S(2)}) collective-permute-start(bf16[256,256]{1,0:T(8,128)(2,1)} %param.5), channel_id=1, source_target_pairs={{0,2},{1,3},{2,4},{3,5},{4,6},{5,7},{6,8},{7,9},{8,10},{9,11},{10,... | collective-permute-start | bytes 393224 | tf_op jit(solution)/shard_map/ppermute | solution.py:10
  11.7 1.4 fusion.9
  13.1 3.1 %collective-permute-done = bf16[256,256]{1,0:T(8,128)(2,1)S(1)} collective-permute-done((bf16[256,256]{1,0:T(8,128)(2,1)}, bf16[256,256]{1,0:T(8,128)(2,1)S(1)}, u32[]{:S(2)}, u32[]{:S(2)}) %collective-permute-start) | collective-permute-done | bytes 131104 | tf_op jit(solution)/shard_map/ppermute | solution.py:10
  16.2 1.3 fusion
  17.6 0.4 multiply_convert_fusion.1
  18.1 0.1 convert_reduce_fusion
  18.2 0.3 copy-done.2
  18.5 0.3 convolution_bitcast_fusion
  18.8 0.1 reshape.31
  18.9 0.7 pad_slice_fusion
  19.6 0.3 fusion.11
  19.9 0.3 convolution_bitcast_fusion.1
  20.3 1.5 pad_maximum_fusion.1
  21.7 1.7 reshape.29
  23.5 2.6 pad_maximum_fusion
  26.1 0.0 reduce-scatter.4.cloned.1.call-update
  26.1 0.0 all-reduce.4.cloned.1.call-start
  26.2 0.1 pad_maximum_fusion.2
  26.3 13.1 %collective-permute-start.1 = (bf16[256,1024]{1,0:T(8,128)(2,1)S(1)}, bf16[256,1024]{1,0:T(8,128)(2,1)S(1)}, u32[]{:S(2)}, u32[]{:S(2)}) collective-permute-start(bf16[256,1024]{1,0:T(8,128)(2,1)S(1)} %pad_maximum_fusion.2), channel_id=1, source_target_pairs={{2,0},{3,1},{4,2},{5,3},{6,4},{7,5},{8,6},{9,7},{10,8},{11,9},{12,... | collective-permute-start | bytes 1572872 | tf_op jit(solution)/shard_map/ppermute | solution.py:10
  39.4 0.9 fusion.1
  40.2 0.3 convolution_add_fusion.3
  40.6 116.4 %reduce-scatter.4.cloned.1.call-done = f32[168,128]{1,0:T(8,128)} async-done(((f32[5376,128]{1,0:T(8,128)}), f32[168,128]{1,0:T(8,128)}) %reduce-scatter.4.cloned.1.call-update) | async-done | bytes 86032
  157.0 0.0 all-reduce.4.cloned.1.call-update
  157.1 1.0 fusion.2
  158.1 138.4 %all-reduce.4.cloned.1.call-done = f32[168,128]{1,0:T(8,128)} async-done(((f32[168,128]{1,0:T(8,128)}), f32[168,128]{1,0:T(8,128)}) %all-reduce.4.cloned.1.call-update) | async-done | bytes 86032 | tf_op jit(solution)/shard_map/psum | solution.py:79
  296.5 0.8 slice.36
  297.3 0.6 reshape.33
  298.0 0.7 slice.38
  298.7 0.6 reshape.34
  299.3 1.2 slice_bitcast_fusion
  (14 shorter events, 0.1 us)
Async XLA Ops:
  7.2 10.4 %copy-start = (bf16[512,256]{1,0:T(8,128)(2,1)S(1)}, bf16[512,256]{1,0:T(8,128)(2,1)}, u32[]{:S(2)}) copy-start(bf16[512,256]{1,0:T(8,128)(2,1)} %param.9) | copy-start | bytes 786436
  7.2 10.4 %copy-start.5 = (bf16[256,256]{1,0:T(8,128)(2,1)S(1)}, bf16[256,256]{1,0:T(8,128)(2,1)}, u32[]{:S(2)}) copy-start(bf16[256,256]{1,0:T(8,128)(2,1)} %param.6) | copy-start | bytes 393220
  7.2 149.8 %reduce-scatter.4.cloned.1.call-start = ((), (), s32[]{:S(2)}) async-start(), calls=%async_computation.2 | async-start | bytes 2838528
  7.2 9.0 %collective-permute-start = (bf16[256,256]{1,0:T(8,128)(2,1)}, bf16[256,256]{1,0:T(8,128)(2,1)S(1)}, u32[]{:S(2)}, u32[]{:S(2)}) collective-permute-start(bf16[256,256]{1,0:T(8,128)(2,1)} %param.5), channel_id=1, source_target_pairs={{0,2},{1,3},{2,4},{3,5},{4,6},{5,7},{6,8},{7,9},{8,10},{9,11},{10,... | collective-permute-start | bytes 393224 | tf_op jit(solution)/shard_map/ppermute | solution.py:10
  17.6 0.9 copy-start.2
  18.1 2.2 copy-start.3
  26.1 13.2 %copy-start.4 = (bf16[256,512]{1,0:T(8,128)(2,1)S(1)}, bf16[256,512]{1,0:T(8,128)(2,1)}, u32[]{:S(2)}) copy-start(bf16[256,512]{1,0:T(8,128)(2,1)} %copy-done.3) | copy-start | bytes 786436
  26.1 14.1 %copy-start.1 = (bf16[512,1024]{1,0:T(8,128)(2,1)S(1)}, bf16[512,1024]{1,0:T(8,128)(2,1)}, u32[]{:S(2)}) copy-start(bf16[512,1024]{1,0:T(8,128)(2,1)} %param.7) | copy-start | bytes 3145732
  26.1 14.1 %copy-start.6 = (bf16[256,256]{1,0:T(8,128)(2,1)S(1)}, bf16[256,256]{1,0:T(8,128)(2,1)}, u32[]{:S(2)}) copy-start(bf16[256,256]{1,0:T(8,128)(2,1)} %param.6) | copy-start | bytes 393220
  26.1 270.3 %all-reduce.4.cloned.1.call-start = ((), (), s32[]{:S(2)}) async-start(), calls=%async_computation.1 | async-start | bytes 172032 | tf_op jit(solution)/shard_map/psum | solution.py:79
  26.3 130.8 %collective-permute-start.1 = (bf16[256,1024]{1,0:T(8,128)(2,1)S(1)}, bf16[256,1024]{1,0:T(8,128)(2,1)S(1)}, u32[]{:S(2)}, u32[]{:S(2)}) collective-permute-start(bf16[256,1024]{1,0:T(8,128)(2,1)S(1)} %pad_maximum_fusion.2), channel_id=1, source_target_pairs={{2,0},{3,1},{4,2},{5,3},{6,4},{7,5},{8,6},{9,7},{10,8},{11,9},{12,... | collective-permute-start | bytes 1572872 | tf_op jit(solution)/shard_map/ppermute | solution.py:10
Sparse Core Ops, SparseCore 0:
  26.3 130.7 reduce-scatter.3
  159.9 136.4 all-reduce.3
where the time goes:
time: 308 us; the launch traced here: 307 us
  waiting for transfers between devices  258 us (84%)
  starting transfers between devices  17.6 us (6%)
  between operations  14.2 us (5%)
  local copies, waits for them, and re-layouts  6.88 us (2%)
  matrix products  6.37 us (2%)
  other arithmetic  4.29 us (1%)
    psum x1, waiting for transfers between devices, per_device(): mine = lax.psum(mine, 'grp')  138 us
    unnamed x3, waiting for transfers between devices  116 us
    ppermute x2, starting transfers between devices, from_behind(): return lax.ppermute(array, axis, pairs)  17.5 us
  transfers between devices with their start and end apart: 4, of which 3 were waited for; matrix products, arithmetic and copies ran while one was open for 1% of the time, Pallas kernels for 0%

commit v1 on v0

--- a/solution.py
+++ b/solution.py
@@ -2,6 +2,12 @@
 import jax.numpy as jnp
 from jax import lax
 from jax.sharding import PartitionSpec as P
+
+
+def gather_and_add(shard, mesh_axis):
+    shards = lax.all_gather(shard, mesh_axis, axis=0, tiled=False)
+    result = shards.sum(axis=0)
+    return result
 
 
 def from_behind(array, axis, by):
@@ -76,7 +82,7 @@
         axis=1,
     ).reshape(groups * (taps_r + out_r + bias_r), lanes)
     mine = lax.psum_scatter(packed, "seq", scatter_dimension=0, tiled=True)
-    mine = lax.psum(mine, "grp")
+    mine = gather_and_add(mine, "grp")
     grad_taps = mine[:taps_r].reshape(rows_taps, part_taps.shape[1])
     grad_out = mine[taps_r : taps_r + out_r].reshape(rows_out, part_out.shape[1])
     grad_bias = mine[taps_r + out_r, :share_bias]

time: 308 us -> 242 us (0.79)
  waiting for transfers between devices: 258 us -> 202 us
  starting transfers between devices: 17.6 us -> 8.3 us
    psum x1 -> x0, waiting for transfers between devices: 138 us -> none  [per_device(): mine = lax.psum(mine, 'grp')]
    all_gather x0 -> x1, waiting for transfers between devices: none -> 59.5 us  [gather_and_add(): shards = lax.all_gather(shard, mesh_axis, axis=0, tiled=False)]
    unnamed x3, waiting for transfers between devices: 116 us -> 131 us
    ppermute x2, starting transfers between devices: 17.5 us -> 8.22 us  [from_behind(): return lax.ppermute(array, axis, pairs)]
    ppermute x2, waiting for transfers between devices: 3.09 us -> 11.5 us  [from_behind(): return lax.ppermute(array, axis, pairs)]
  transfers between devices with their start and end apart: 4 -> 4, of which waited for: 3 -> 4; matrix products, arithmetic and copies ran while one was open for 1% -> 2% of each run, Pallas kernels for 0% -> 0%
where the time goes in v1:
time: 242 us; the launch traced here: 241 us
  waiting for transfers between devices  202 us (83%)
  between operations  14.2 us (6%)
  starting transfers between devices  8.3 us (3%)
  matrix products  6.36 us (3%)
  other arithmetic  5.7 us (2%)
  local copies, waits for them, and re-layouts  4.65 us (2%)
    unnamed x3, waiting for transfers between devices  131 us
    all_gather x1, waiting for transfers between devices, gather_and_add(): shards = lax.all_gather(shard, mesh_axis, axis=0, tiled=False)  59.5 us
    ppermute x2, waiting for transfers between devices, from_behind(): return lax.ppermute(array, axis, pairs)  11.5 us
    ppermute x2, starting transfers between devices, from_behind(): return lax.ppermute(array, axis, pairs)  8.22 us
  transfers between devices with their start and end apart: 4, of which 4 were waited for; matrix products, arithmetic and copies ran while one was open for 2% of the time, Pallas kernels for 0%

profile of v1, /device:TPU:6, one launch (start us, length us, event | category | flops | bytes accessed | tf_op | source)
XLA Modules:
  0.0 241.3 jit_solution(12903264072030874815)
XLA Ops:
  7.2 0.0 copy-start
  7.2 0.0 reduce-scatter.4.cloned.1.call-start
  7.2 4.5 %collective-permute-start = (bf16[256,256]{1,0:T(8,128)(2,1)}, bf16[256,256]{1,0:T(8,128)(2,1)S(1)}, u32[]{:S(2)}, u32[]{:S(2)}) collective-permute-start(bf16[256,256]{1,0:T(8,128)(2,1)} %param.5), channel_id=1, source_target_pairs={{0,2},{1,3},{2,4},{3,5},{4,6},{5,7},{6,8},{7,9},{8,10},{9,11},{10,... | collective-permute-start | bytes 393224 | tf_op jit(solution)/shard_map/ppermute | solution.py:16
  11.7 1.4 fusion.9
  13.1 3.1 %collective-permute-done = bf16[256,256]{1,0:T(8,128)(2,1)S(1)} collective-permute-done((bf16[256,256]{1,0:T(8,128)(2,1)}, bf16[256,256]{1,0:T(8,128)(2,1)S(1)}, u32[]{:S(2)}, u32[]{:S(2)}) %collective-permute-start) | collective-permute-done | bytes 131104 | tf_op jit(solution)/shard_map/ppermute | solution.py:16
  16.2 1.3 fusion
  17.6 0.4 multiply_convert_fusion.1
  18.1 0.1 convert_reduce_fusion
  18.2 0.3 copy-done.2
  18.5 0.3 convolution_bitcast_fusion
  18.8 0.1 reshape.31
  18.9 0.7 pad_slice_fusion
  19.6 0.3 fusion.11
  19.9 0.3 convolution_bitcast_fusion.1
  20.3 1.5 pad_maximum_fusion.1
  21.7 1.7 reshape.29
  23.5 2.6 %pad_maximum_fusion = f32[32,168,128]{2,1,0:T(8,128)} fusion(f32[32,8,128]{2,1,0:T(8,128)} %pad_slice_fusion, f32[32,32,128]{2,1,0:T(8,128)S(1)} %reshape.30, f32[32,128,128]{2,1,0:T(8,128)S(1)} %reshape.29), kind=kLoop, calls=%fused_computation | loop fusion | flops 1376256 | bytes 5505024 | tf_op jit(solution)/shard_map/concatenate | solution.py:76
  26.1 0.0 reduce-scatter.4.cloned.1.call-update
  26.1 0.0 all-gather.3.cloned.1.call-start
  26.2 131.0 %reduce-scatter.4.cloned.1.call-done = f32[168,128]{1,0:T(8,128)} async-done(((f32[5376,128]{1,0:T(8,128)}), f32[168,128]{1,0:T(8,128)}) %reduce-scatter.4.cloned.1.call-update) | async-done | bytes 86032
  157.2 0.0 all-gather.3.cloned.1.call-update
  157.2 0.1 pad_maximum_fusion.2
  157.3 3.8 %collective-permute-start.1 = (bf16[256,1024]{1,0:T(8,128)(2,1)S(1)}, bf16[256,1024]{1,0:T(8,128)(2,1)S(1)}, u32[]{:S(2)}, u32[]{:S(2)}) collective-permute-start(bf16[256,1024]{1,0:T(8,128)(2,1)S(1)} %pad_maximum_fusion.2), channel_id=1, source_target_pairs={{2,0},{3,1},{4,2},{5,3},{6,4},{7,5},{8,6},{9,7},{10,8},{11,9},{12,... | collective-permute-start | bytes 1572872 | tf_op jit(solution)/shard_map/ppermute | solution.py:16
  161.1 0.9 fusion.1
  161.9 0.3 convolution_add_fusion.3
  162.3 8.5 %collective-permute-done.1 = bf16[256,1024]{1,0:T(8,128)(2,1)S(1)} collective-permute-done((bf16[256,1024]{1,0:T(8,128)(2,1)S(1)}, bf16[256,1024]{1,0:T(8,128)(2,1)S(1)}, u32[]{:S(2)}, u32[]{:S(2)}) %collective-permute-start.1) | collective-permute-done | bytes 524320 | tf_op jit(solution)/shard_map/ppermute | solution.py:16
  170.7 1.0 fusion.2
  171.7 59.5 %all-gather.3.cloned.1.call-done = f32[2688,128]{1,0:T(8,128)} async-done(((f32[168,128]{1,0:T(8,128)}), f32[2688,128]{1,0:T(8,128)}) %all-gather.3.cloned.1.call-update) | async-done | bytes 1376272 | tf_op jit(solution)/shard_map/all_gather | solution.py:8
  231.2 1.4 reduce_sum.19
  232.6 0.5 slice_bitcast_fusion
  233.2 0.6 reshape.33
  233.8 0.6 reshape.34
  (15 shorter events, 0.1 us)
Async XLA Ops:
  7.2 10.4 %copy-start = (bf16[512,256]{1,0:T(8,128)(2,1)S(1)}, bf16[512,256]{1,0:T(8,128)(2,1)}, u32[]{:S(2)}) copy-start(bf16[512,256]{1,0:T(8,128)(2,1)} %param.9) | copy-start | bytes 786436
  7.2 10.4 %copy-start.5 = (bf16[256,256]{1,0:T(8,128)(2,1)S(1)}, bf16[256,256]{1,0:T(8,128)(2,1)}, u32[]{:S(2)}) copy-start(bf16[256,256]{1,0:T(8,128)(2,1)} %param.6) | copy-start | bytes 393220
  7.2 150.0 %reduce-scatter.4.cloned.1.call-start = ((), (), s32[]{:S(2)}) async-start(), calls=%async_computation.2 | async-start | bytes 2838528
  7.2 9.0 %collective-permute-start = (bf16[256,256]{1,0:T(8,128)(2,1)}, bf16[256,256]{1,0:T(8,128)(2,1)S(1)}, u32[]{:S(2)}, u32[]{:S(2)}) collective-permute-start(bf16[256,256]{1,0:T(8,128)(2,1)} %param.5), channel_id=1, source_target_pairs={{0,2},{1,3},{2,4},{3,5},{4,6},{5,7},{6,8},{7,9},{8,10},{9,11},{10,... | collective-permute-start | bytes 393224 | tf_op jit(solution)/shard_map/ppermute | solution.py:16
  17.6 0.9 copy-start.2
  18.1 1.8 copy-start.3
  26.1 134.9 %copy-start.4 = (bf16[256,512]{1,0:T(8,128)(2,1)S(1)}, bf16[256,512]{1,0:T(8,128)(2,1)}, u32[]{:S(2)}) copy-start(bf16[256,512]{1,0:T(8,128)(2,1)} %copy-done.3) | copy-start | bytes 786436
  26.1 135.8 %copy-start.1 = (bf16[512,1024]{1,0:T(8,128)(2,1)S(1)}, bf16[512,1024]{1,0:T(8,128)(2,1)}, u32[]{:S(2)}) copy-start(bf16[512,1024]{1,0:T(8,128)(2,1)} %param.7) | copy-start | bytes 3145732
  26.1 135.8 %copy-start.6 = (bf16[256,256]{1,0:T(8,128)(2,1)S(1)}, bf16[256,256]{1,0:T(8,128)(2,1)}, u32[]{:S(2)}) copy-start(bf16[256,256]{1,0:T(8,128)(2,1)} %param.6) | copy-start | bytes 393220
  26.1 205.1 %all-gather.3.cloned.1.call-start = ((), (), s32[]{:S(2)}) async-start(), calls=%async_computation.1 | async-start | bytes 1462272 | tf_op jit(solution)/shard_map/all_gather | solution.py:8
  157.3 13.5 %collective-permute-start.1 = (bf16[256,1024]{1,0:T(8,128)(2,1)S(1)}, bf16[256,1024]{1,0:T(8,128)(2,1)S(1)}, u32[]{:S(2)}, u32[]{:S(2)}) collective-permute-start(bf16[256,1024]{1,0:T(8,128)(2,1)S(1)} %pad_maximum_fusion.2), channel_id=1, source_target_pairs={{2,0},{3,1},{4,2},{5,3},{6,4},{7,5},{8,6},{9,7},{10,8},{11,9},{12,... | collective-permute-start | bytes 1572872 | tf_op jit(solution)/shard_map/ppermute | solution.py:16
Sparse Core Ops, SparseCore 0:
  26.3 130.8 reduce-scatter.3
  159.3 71.9 all-gather.2
